TPU v7x, 512 devices: a whole 4x8x8 slice. The times are simulated.
512 devices in a mesh: dp: 32 (over y, x), tensor: 16 (over z, core).
Axes of the slice: x: 4, y: 8, z: 8, core: 2. Of those that a mesh axis runs over, the one named last changes fastest.
Arguments:
- patch_rows: bfloat16 [32, 3072, 1792], P('dp', 'tensor'), may hold values from -6 to 6
- send_rows: int32 [32, 16, 32, 6], P('dp', 'tensor'), may hold values from 0 to 192, as said below
- take_rows: int32 [32, 2048], P('dp', 'tensor'), may hold values from 0 to 191, as said below
- segments: int32 [32, 2048], P('dp', 'tensor'), may hold values from 0 to 41, never falling along the last dimension, each value on 1 to 96 neighbouring positions
- norm_gain: float32 [1792], replicated, may hold values from 0.5 to 5
- qkv_weight: bfloat16 [1792, 2688], P('tensor'), may hold values from -0.125 to 0.125
- out_weight: bfloat16 [896, 1792], P('tensor'), may hold values from -0.1875 to 0.1875
- grad_out: bfloat16 [32, 2048, 1792], P('dp', 'tensor'), may hold values from -6 to 6
Outputs:
- layer_out: bfloat16 [32, 2048, 1792], P('dp', 'tensor')
- patch_grad: bfloat16 [32, 3072, 1792], P('dp', 'tensor')
Inputs may be any that keep to these rules, and one draw needn't show every extreme that they name: `send_rows`: for each source device (s, t) the entries below 192 are distinct, 128 in all; for each group they fill slots from 0 on, the rest being 192; some device sends 6 rows to some group. `take_rows`: for each g and t the 128 entries are distinct and name exactly the slots s * 6 + c that hold a row (c below the number of rows that device (s, t) sends to group g). `segments`: along each row the ids never fall and each id covers 1 to 96 positions.
All inputs are finite; a program needn't handle non-finite values.
Results may differ from a plain program's by a relative error of at most 0.009.
The roundings to bfloat16 on the way count: a program that leaves them out, or rounds other values in their place, can miss the bound.
Values may be sent and summed in bfloat16 or wider, within the bound.
No kernel may reach another device: no remote copies, remote signals or barrier semaphores. Data moves between devices by JAX's collectives and lax.ppermute only.
A program may use at most 128 MiB of HBM per device.

v0:
```python
import jax
import jax.numpy as jnp
from jax import lax
from jax.sharding import PartitionSpec as P

HD = 112
HEADS = 8
MOST = 96


def extended(block, sides, width):
    for axis, dim in sides:
        count = lax.axis_size(axis)
        forward = [(i, i + 1) for i in range(count - 1)]
        backward = [(target, source) for source, target in forward]
        low = lax.ppermute(
            lax.slice_in_dim(block, block.shape[dim] - width, None, axis=dim), axis, forward
        )
        high = lax.ppermute(lax.slice_in_dim(block, 0, width, axis=dim), axis, backward)
        block = jnp.concatenate([low, block, high], axis=dim)
    return block


def normalize(rows_in, norm_gain):
    values = rows_in.astype(jnp.float32)
    center = values - jnp.mean(values, axis=-1, keepdims=True)
    inv_dev = lax.rsqrt(jnp.mean(center * center, axis=-1, keepdims=True) + 1e-06)
    unit_rows = center * inv_dev
    return (values, unit_rows, inv_dev, (unit_rows * norm_gain).astype(jnp.bfloat16))


def split_heads(rows_in):
    return rows_in.reshape(rows_in.shape[0], HEADS, HD)


def attend(queries, keyval, seg_query, seg_key):
    all_heads = HEADS * HD
    score_scale = HD ** (-0.5)
    query_heads = split_heads(queries)
    key_heads = split_heads(keyval[:, :all_heads])
    value_heads = split_heads(keyval[:, all_heads:])
    scores = (
        jnp.einsum("qhd,khd->hqk", query_heads, key_heads, preferred_element_type=jnp.float32)
        * score_scale
    )
    same_chart = seg_query[:, None] == seg_key[None, :]
    scores = jnp.where(same_chart[None], scores, -jnp.inf)
    row_max = jnp.max(scores, axis=2, keepdims=True)
    exp_scores = jnp.exp(scores - row_max)
    row_sum = jnp.sum(exp_scores, axis=2, keepdims=True)
    attn_probs = exp_scores / row_sum
    prob_low = attn_probs.astype(jnp.bfloat16)
    attended = jnp.einsum("hqk,khd->qhd", prob_low, value_heads, preferred_element_type=jnp.float32)
    return (
        attn_probs,
        prob_low,
        attended.astype(jnp.bfloat16).reshape(queries.shape[0], all_heads),
        row_max + jnp.log(row_sum),
    )


def local(patch_rows, send_rows, take_rows, segments, norm_gain, qkv_weight, out_weight, grad_out):
    groups = lax.axis_size("dp")
    src_count = patch_rows.shape[1]
    features = patch_rows.shape[2]
    slot_count = send_rows.shape[3]
    own_rows = take_rows.shape[1]
    all_heads = HEADS * HD
    score_scale = HD ** (-0.5)
    patches = patch_rows[0]
    send_flat = send_rows.reshape(groups * slot_count)
    outgoing = jnp.take(patches, send_flat, axis=0, mode="fill", fill_value=0).reshape(
        groups, slot_count, features
    )
    incoming = lax.all_to_all(outgoing, "dp", split_axis=0, concat_axis=0, tiled=True).reshape(
        groups * slot_count, features
    )
    pick_rows = take_rows[0]
    packed = jnp.take(incoming, pick_rows, axis=0)
    full_qkv, full_out = (
        lax.all_gather(qkv_weight, "tensor", axis=0, tiled=True),
        lax.all_gather(out_weight, "tensor", axis=0, tiled=True),
    )
    values, unit_rows, inv_dev, normed = normalize(packed, norm_gain)
    projected = jnp.dot(normed, full_qkv, preferred_element_type=jnp.float32).astype(jnp.bfloat16)
    queries = projected[:, :all_heads]
    keyval = projected[:, all_heads:]
    seg_plus = segments[0] + 1
    wide_kv, wide_seg = (
        extended(keyval, (("tensor", 0),), MOST),
        extended(seg_plus, (("tensor", 0),), MOST),
    )
    attn_probs, prob_low, attended, log_norm = attend(queries, wide_kv, seg_plus, wide_seg)
    layer_out = (values + jnp.dot(attended, full_out, preferred_element_type=jnp.float32)).astype(
        jnp.bfloat16
    )
    grad_rows = grad_out[0]
    grad_att = lax.dot_general(
        grad_rows, full_out, (((1,), (1,)), ((), ())), preferred_element_type=jnp.float32
    ).astype(jnp.bfloat16)
    query_heads = split_heads(queries)
    grad_heads = split_heads(grad_att)
    wide_keys = split_heads(wide_kv[:, :all_heads])
    wide_values = split_heads(wide_kv[:, all_heads:])
    dprobs = jnp.einsum("qhd,khd->hqk", grad_heads, wide_values, preferred_element_type=jnp.float32)
    row_inner = jnp.sum(attn_probs * dprobs, axis=2, keepdims=True)
    dscore = (attn_probs * (dprobs - row_inner) * score_scale).astype(jnp.bfloat16)
    grad_query = jnp.einsum(
        "hqk,khd->qhd", dscore, wide_keys, preferred_element_type=jnp.float32
    ).reshape(own_rows, all_heads)
    window_rows = wide_kv.shape[0]
    grad_key = jnp.einsum("hqk,qhd->khd", dscore, query_heads, preferred_element_type=jnp.float32)
    grad_value = jnp.einsum(
        "hqk,qhd->khd", prob_low, grad_heads, preferred_element_type=jnp.float32
    )
    grad_window = jnp.concatenate(
        [grad_key.reshape(window_rows, all_heads), grad_value.reshape(window_rows, all_heads)],
        axis=1,
    )
    center = grad_window[MOST : MOST + own_rows]
    rim_parts = jnp.concatenate([grad_window[:MOST], grad_window[MOST + own_rows :]], axis=0)
    arrived = extended(rim_parts, (("tensor", 0),), MOST)
    center = center.at[:MOST].add(arrived[:MOST])
    center = center.at[own_rows - MOST :].add(arrived[3 * MOST :])
    grad_proj = jnp.concatenate([grad_query, center], axis=1).astype(jnp.bfloat16)
    grad_normed = lax.dot_general(
        grad_proj, full_qkv, (((1,), (1,)), ((), ())), preferred_element_type=jnp.float32
    )
    scaled = grad_normed * norm_gain
    grad_unit = (
        scaled
        - jnp.mean(scaled, axis=-1, keepdims=True)
        - unit_rows * jnp.mean(scaled * unit_rows, axis=-1, keepdims=True)
    )
    grad_packed = (grad_rows.astype(jnp.float32) + inv_dev * grad_unit).astype(jnp.bfloat16)
    back_slots = (
        jnp.zeros((groups * slot_count, features), jnp.bfloat16).at[pick_rows].set(grad_packed)
    )
    back_slots = back_slots.reshape(groups, slot_count, features)
    returned = lax.all_to_all(back_slots, "dp", split_axis=0, concat_axis=0, tiled=True).reshape(
        groups * slot_count, features
    )
    patch_grad = (
        jnp.zeros((src_count + 1, features), jnp.bfloat16).at[send_flat].add(returned)[:src_count]
    )
    return (layer_out[None], patch_grad[None])


def solution(mesh):
    return jax.shard_map(
        local,
        mesh=mesh,
        in_specs=(
            P("dp", "tensor", None),
            P("dp", "tensor", None, None),
            P("dp", "tensor"),
            P("dp", "tensor"),
            P(),
            P("tensor", None),
            P("tensor", None),
            P("dp", "tensor", None),
        ),
        out_specs=(P("dp", "tensor", None), P("dp", "tensor", None)),
        check_vma=False,
    )
```

profile of v0, /device:TPU:1, one launch (start us, length us, event | category | flops | bytes accessed | tf_op | source)
XLA Modules:
  0.0 227.3 jit_solution(14492804435034020752)
XLA Ops:
  12.9 10.6 %all-to-all-start = ((bf16[32,6,1792]{2,1,0:T(8,128)(2,1)}), bf16[32,6,1792]{2,1,0:T(8,128)(2,1)S(1)}, u32[]{:S(2)}, u32[]{:S(2)}) async-start(bf16[32,6,1792]{2,1,0:T(8,128)(2,1)} %broadcast_select_fusion), calls=%async_computation | async-start | bytes 1835008 | tf_op jit(solution)/shard_map/all_to_all | solution.py:75
  23.6 4.8 %collective-permute-start.2 = (s32[96]{0:T(128)S(1)}, s32[96]{0:T(128)S(1)}, u32[]{:S(2)}, u32[]{:S(2)}) collective-permute-start(s32[96]{0:T(128)S(1)} %get-tuple-element.36), channel_id=1, source_target_pairs={{0,1},{1,2},{2,3},{3,4},{4,5},{5,6},{6,7},{7,8},{8,9},{9,10},{10,1... | collective-permute-start | bytes 1160 | tf_op jit(solution)/shard_map/ppermute | solution.py:16
  28.5 1.9 collective-permute-start.3
  30.5 3.3 %collective-permute-done.3 = s32[96]{0:T(128)S(1)} collective-permute-done((s32[96]{0:T(128)S(1)}, s32[96]{0:T(128)S(1)}, u32[]{:S(2)}, u32[]{:S(2)}) %collective-permute-start.3) | collective-permute-done | bytes 416 | tf_op jit(solution)/shard_map/ppermute | solution.py:19
  33.8 13.2 %all-to-all-done = bf16[32,6,1792]{2,1,0:T(8,128)(2,1)S(1)} async-done(((bf16[32,6,1792]{2,1,0:T(8,128)(2,1)}), bf16[32,6,1792]{2,1,0:T(8,128)(2,1)S(1)}, u32[]{:S(2)}, u32[]{:S(2)}) %all-to-all-start) | async-done | bytes 688160 | tf_op jit(solution)/shard_map/all_to_all | solution.py:75
  48.7 32.5 %all-gather.3.cloned.1.call-done = bf16[1792,2688]{1,0:T(8,128)(2,1)} async-done(((bf16[112,2688]{1,0:T(8,128)(2,1)}), bf16[1792,2688]{1,0:T(8,128)(2,1)}) %all-gather.3.cloned.1.call-update) | async-done | bytes 9633808 | tf_op jit(solution)/shard_map/all_gather | solution.py:81
  81.3 5.4 %convolution_convert_fusion = bf16[128,2688]{1,0:T(8,128)(2,1)S(1)} fusion(bf16[1792,2688]{1,0:T(8,128)(2,1)} %all-gather.3.cloned.1.call-done, f32[1792]{0:T(1024)S(1)} %copy-done.10, f32[128]{0:T(128)S(1)} %add_rsqrt_fusion, f32[128]{0:T(128)S(1)} %broadcast_multiply_fusion.2, bf16[128,1792]{1,0:T(8,128)(2,1)S(1)} %gather_fusion.1, ...), kind=kOutput, calls=%fused_computation.6 | convolution fusion | flops 1234845696 | bytes 10788992 | tf_op jit(solution)/shard_map/dot_general | solution.py:85
  87.6 1.9 collective-permute-start
  89.5 2.4 %collective-permute-start.1 = (bf16[96,1792]{1,0:T(8,128)(2,1)}, bf16[96,1792]{1,0:T(8,128)(2,1)}, u32[]{:S(2)}, u32[]{:S(2)}) collective-permute-start(bf16[96,1792]{1,0:T(8,128)(2,1)} %get-tuple-element.33), channel_id=1, source_target_pairs={{1,0},{2,1},{3,2},{4,3},{5,4},{6,5},{7,6},{8,7},{9,8},{10,9},{11,1... | collective-permute-start | bytes 1032200 | tf_op jit(solution)/shard_map/ppermute | solution.py:19
  92.1 34.0 %all-gather.5.cloned.1.call-done = bf16[896,1792]{1,0:T(8,128)(2,1)} async-done(((bf16[56,1792]{1,0:T(8,128)(2,1)}), bf16[896,1792]{1,0:T(8,128)(2,1)}) %all-gather.5.cloned.1.call-update) | async-done | bytes 3211280 | tf_op jit(solution)/shard_map/all_gather | solution.py:82
  126.0 3.0 %convolution_convert_fusion.1 = bf16[128,896]{1,0:T(8,128)(2,1)S(1)} fusion(bf16[896,1792]{1,0:T(8,128)(2,1)} %all-gather.5.cloned.1.call-done, bf16[1,128,1792]{2,1,0:T(8,128)(2,1)S(1)} %copy-done.4), kind=kOutput, calls=%fused_computation.28 | convolution fusion | flops 411156480 | bytes 3899392 | tf_op jit(solution)/shard_map/dot_general | solution.py:98
  131.3 1.6 reshape.258
  134.0 3.2 %fusion.98 = (f32[8,128]{1,0:T(8,128)S(1)}, f32[8,128,320]{1,2,0:T(8,128)}) fusion(pred[128,320]{0,1:T(8,128)(4,1)S(1)} %broadcast_compare_fusion, bf16[128,8,112]{0,2,1:T(8,128)(2,1)} %bitcast.59, bf16[320,8,112]{2,1,0:T(8,128)(2,1)} %reshape.258), kind=kOutput, calls=%fused_computation.111 | convolution fusion | flops 74711360 | bytes 2158592 | tf_op jit(solution)/shard_map/sub | solution.py:49
  137.3 3.0 %convolution_bitcast_fusion = f32[320,8,112]{2,0,1:T(8,128)} fusion(bf16[128,8,112]{0,2,1:T(8,128)(2,1)S(1)} %bitcast.58, f32[8,128]{1,0:T(8,128)S(1)} %get-tuple-element.40, pred[128,320]{0,1:T(8,128)(4,1)S(1)} %broadcast_compare_fusion, bf16[128,8,112]{0,2,1:T(8,128)(2,1)} %bitcast.60, bf16[320,8,112]{2,1,0:T(8,128)(2,1)} %reshape.258), kind=kOutput, calls=%fused_computation.17 | convolution fusion | flops 148440384 | bytes 2224128 | tf_op jit(solution)/shard_map/hqk,qhd->khd/dot_general | solution.py:113
  140.3 3.4 %convolution_bitcast_fusion.1 = f32[320,8,112]{2,0,1:T(8,128)} fusion(bf16[128,8,112]{0,2,1:T(8,128)(2,1)S(1)} %bitcast.61, f32[8,128,320]{1,2,0:T(8,128)S(1)} %fusion.41, f32[8,128,320]{1,2,0:T(8,128)} %get-tuple-element.41, f32[8,128]{1,0:T(8,128)S(1)} %get-tuple-element.40), kind=kOutput, calls=%fused_computation.18 | convolution fusion | flops 75695424 | bytes 4001792 | tf_op jit(solution)/shard_map/hqk,qhd->khd/dot_general | solution.py:112
  143.7 2.1 copy.28
  147.2 2.1 copy.29
  149.3 1.4 reshape.263
  153.6 3.4 %collective-permute-start.4 = (f32[96,1792]{1,0:T(8,128)}, f32[96,1792]{1,0:T(8,128)}, u32[]{:S(2)}, u32[]{:S(2)}) collective-permute-start(f32[96,1792]{1,0:T(8,128)} %get-tuple-element.29), channel_id=1, source_target_pairs={{0,1},{1,2},{2,3},{3,4},{4,5},{5,6},{6,7},{7,8},{8,9},{9,10},{10,1... | collective-permute-start | bytes 2064392 | tf_op jit(solution)/shard_map/ppermute | solution.py:16
  158.0 1.9 collective-permute-start.5
  159.9 4.3 %fusion.17 = bf16[8,112,128]{2,1,0:T(8,128)(2,1)} fusion(f32[8,128,320]{1,2,0:T(8,128)} %copy-done.6, bf16[320,8,112]{2,1,0:T(8,128)(2,1)} %reshape.258, f32[8,128,320]{1,2,0:T(8,128)} %get-tuple-element.41, f32[8,128]{1,0:T(8,128)S(1)} %get-tuple-element.40), kind=kOutput, calls=%fused_computation.27 | convolution fusion | flops 75810112 | bytes 3428352 | tf_op jit(solution)/shard_map/hqk,khd->qhd/dot_general | solution.py:108
  164.3 1.8 copy.30
  166.0 2.0 fusion.33
  168.1 2.5 %collective-permute-done.5 = f32[96,1792]{1,0:T(8,128)} collective-permute-done((f32[96,1792]{1,0:T(8,128)}, f32[96,1792]{1,0:T(8,128)}, u32[]{:S(2)}, u32[]{:S(2)}) %collective-permute-start.5) | collective-permute-done | bytes 688160 | tf_op jit(solution)/shard_map/ppermute | solution.py:19
  170.6 2.3 fusion.32
  174.1 6.6 %fusion.94 = (f32[128]{0:T(128)S(1)}, f32[128]{0:T(128)S(1)}, f32[128,1792]{1,0:T(8,128)S(1)}) fusion(f32[128]{0:T(128)S(1)} %add_rsqrt_fusion, f32[128]{0:T(128)S(1)} %broadcast_multiply_fusion.2, bf16[128,1792]{1,0:T(8,128)(2,1)S(1)} %gather_fusion.1, pred[128]{0:T(512)(128)(4,1)S(1)} %compare_and_fusion.1, f32[1792]{0:T(1024)S(1)} %copy-done.10, ...), kind=kOutput, calls=%fused_computation.107 | convolution fusion | flops 1236336384 | bytes 11707520 | tf_op jit(solution)/shard_map/dot_general | solution.py:126
  180.7 1.9 scatter_custom_fusion
  183.8 9.4 %all-to-all-start.1 = ((bf16[32,6,1792]{2,1,0:T(8,128)(2,1)}), bf16[32,6,1792]{2,1,0:T(8,128)(2,1)S(1)}, u32[]{:S(2)}, u32[]{:S(2)}) async-start(bf16[32,6,1792]{2,1,0:T(8,128)(2,1)} %reshape.264), calls=%async_computation.1 | async-start | bytes 1835008 | tf_op jit(solution)/shard_map/all_to_all | solution.py:140
  193.2 2.0 convolution_convert_fusion.2
  195.2 3.3 %fusion.3 = bf16[1,128,1792]{2,1,0:T(8,128)(2,1)} fusion(bf16[128,896]{0,1:T(8,128)(2,1)S(1)} %bitcast.64, bf16[896,1792]{1,0:T(8,128)(2,1)} %all-gather.5.cloned.1.call-done, bf16[128,1792]{1,0:T(8,128)(2,1)S(1)} %gather_fusion.1, pred[128]{0:T(512)(128)(4,1)S(1)} %compare_and_fusion.1), kind=kOutput, calls=%fused_computation.10 | convolution fusion | flops 411959296 | bytes 4358272 | tf_op jit(solution)/shard_map/dot_general | solution.py:94
  198.5 17.8 %all-to-all-done.1 = bf16[32,6,1792]{2,1,0:T(8,128)(2,1)S(1)} async-done(((bf16[32,6,1792]{2,1,0:T(8,128)(2,1)}), bf16[32,6,1792]{2,1,0:T(8,128)(2,1)S(1)}, u32[]{:S(2)}, u32[]{:S(2)}) %all-to-all-start.1) | async-done | bytes 688160 | tf_op jit(solution)/shard_map/all_to_all | solution.py:140
  216.5 3.1 %scatter_custom_fusion.1 = bf16[193,1792]{1,0:T(8,128)(2,1)S(1)} fusion(s32[192]{0:T(256)S(1)} %bitcast.66, bf16[192,1792]{1,0:T(8,128)(2,1)S(1)} %reshape.294, bf16[]{:T(256)} %constant.97.clone.1), kind=kCustom, calls=%fused_computation.73 | custom fusion | flops 344064 | bytes 691714 | tf_op jit(solution)/shard_map/scatter-add | solution.py:144
  (75 shorter events, 20.7 us)
Async XLA Ops:
  7.2 3.2 %copy-start = (bf16[1,192,1792]{2,1,0:T(8,128)(2,1)S(1)}, bf16[1,192,1792]{2,1,0:T(8,128)(2,1)}, u32[]{:S(2)}) copy-start(bf16[1,192,1792]{2,1,0:T(8,128)(2,1)} %param.12) | copy-start | bytes 2064388
  7.2 74.1 %all-gather.3.cloned.1.call-start = ((), (), s32[]{:S(2)}) async-start(), calls=%async_computation.2 | async-start | bytes 10235904 | tf_op jit(solution)/shard_map/all_gather | solution.py:81
  7.9 118.1 %all-gather.5.cloned.1.call-start = ((), (), s32[]{:S(2)}) async-start(), calls=%async_computation.3 | async-start | bytes 3411968 | tf_op jit(solution)/shard_map/all_gather | solution.py:82
  12.9 10.6 %copy-start.11 = (s32[1,128]{1,0:T(1,128)S(1)}, s32[1,128]{1,0:T(1,128)}, u32[]{:S(2)}) copy-start(s32[1,128]{1,0:T(1,128)} %param.15) | copy-start | bytes 1540
  12.9 17.5 %copy-start.12 = (s32[1,128]{1,0:T(1,128)S(1)}, s32[1,128]{1,0:T(1,128)}, u32[]{:S(2)}) copy-start(s32[1,128]{1,0:T(1,128)} %param.14) | copy-start | bytes 1540
  12.9 34.1 %all-to-all-start = ((bf16[32,6,1792]{2,1,0:T(8,128)(2,1)}), bf16[32,6,1792]{2,1,0:T(8,128)(2,1)S(1)}, u32[]{:S(2)}, u32[]{:S(2)}) async-start(bf16[32,6,1792]{2,1,0:T(8,128)(2,1)} %broadcast_select_fusion), calls=%async_computation | async-start | bytes 1835008 | tf_op jit(solution)/shard_map/all_to_all | solution.py:75
  23.6 6.8 %collective-permute-start.2 = (s32[96]{0:T(128)S(1)}, s32[96]{0:T(128)S(1)}, u32[]{:S(2)}, u32[]{:S(2)}) collective-permute-start(s32[96]{0:T(128)S(1)} %get-tuple-element.36), channel_id=1, source_target_pairs={{0,1},{1,2},{2,3},{3,4},{4,5},{5,6},{6,7},{7,8},{8,9},{9,10},{10,1... | collective-permute-start | bytes 1160 | tf_op jit(solution)/shard_map/ppermute | solution.py:16
  28.5 5.3 %collective-permute-start.3 = (s32[96]{0:T(128)S(1)}, s32[96]{0:T(128)S(1)}, u32[]{:S(2)}, u32[]{:S(2)}) collective-permute-start(s32[96]{0:T(128)S(1)} %get-tuple-element.37), channel_id=1, source_target_pairs={{1,0},{2,1},{3,2},{4,3},{5,4},{6,5},{7,6},{8,7},{9,8},{10,9},{11,1... | collective-permute-start | bytes 1160 | tf_op jit(solution)/shard_map/ppermute | solution.py:19
  47.2 34.1 %copy-start.10 = (f32[1792]{0:T(1024)S(1)}, f32[1792]{0:T(1024)}, u32[]{:S(2)}) copy-start(f32[1792]{0:T(1024)} %param.16) | copy-start | bytes 21508
  86.7 39.3 %copy-start.4 = (bf16[1,128,1792]{2,1,0:T(8,128)(2,1)S(1)}, bf16[1,128,1792]{2,1,0:T(8,128)(2,1)}, u32[]{:S(2)}) copy-start(bf16[1,128,1792]{2,1,0:T(8,128)(2,1)} %param.19) | copy-start | bytes 1376260
  87.6 42.6 %collective-permute-start = (bf16[96,1792]{1,0:T(8,128)(2,1)}, bf16[96,1792]{1,0:T(8,128)(2,1)S(1)}, u32[]{:S(2)}, u32[]{:S(2)}) collective-permute-start(bf16[96,1792]{1,0:T(8,128)(2,1)} %get-tuple-element.32), channel_id=1, source_target_pairs={{0,1},{1,2},{2,3},{3,4},{4,5},{5,6},{6,7},{7,8},{8,9},{9,10},{10,1... | collective-permute-start | bytes 1032200 | tf_op jit(solution)/shard_map/ppermute | solution.py:16
  89.5 40.6 %collective-permute-start.1 = (bf16[96,1792]{1,0:T(8,128)(2,1)}, bf16[96,1792]{1,0:T(8,128)(2,1)}, u32[]{:S(2)}, u32[]{:S(2)}) collective-permute-start(bf16[96,1792]{1,0:T(8,128)(2,1)} %get-tuple-element.33), channel_id=1, source_target_pairs={{1,0},{2,1},{3,2},{4,3},{5,4},{6,5},{7,6},{8,7},{9,8},{10,9},{11,1... | collective-permute-start | bytes 1032200 | tf_op jit(solution)/shard_map/ppermute | solution.py:19
  133.7 3.6 %copy-start.2 = (bf16[320,8,112]{2,1,0:T(8,128)(2,1)}, bf16[320,8,112]{2,1,0:T(8,128)(2,1)S(1)}, u32[]{:S(2)}) copy-start(bf16[320,8,112]{2,1,0:T(8,128)(2,1)S(1)} %reshape.256) | copy-start | bytes 1720324
  134.0 6.3 %copy-start.6 = (f32[8,128,320]{1,2,0:T(8,128)}, f32[8,128,320]{1,2,0:T(8,128)S(1)}, u32[]{:S(2)}) copy-start(f32[8,128,320]{1,2,0:T(8,128)S(1)} %fusion.41) | copy-start | bytes 3932164
  137.3 3.0 %copy-start.7 = (bf16[128,896]{0,1:T(8,128)(2,1)S(1)}, bf16[128,896]{0,1:T(8,128)(2,1)}, u32[]{:S(2)}) copy-start(bf16[128,896]{0,1:T(8,128)(2,1)} %copy.22) | copy-start | bytes 688132
  150.7 1.6 copy-start.1
  153.6 12.5 %collective-permute-start.4 = (f32[96,1792]{1,0:T(8,128)}, f32[96,1792]{1,0:T(8,128)}, u32[]{:S(2)}, u32[]{:S(2)}) collective-permute-start(f32[96,1792]{1,0:T(8,128)} %get-tuple-element.29), channel_id=1, source_target_pairs={{0,1},{1,2},{2,3},{3,4},{4,5},{5,6},{6,7},{7,8},{8,9},{9,10},{10,1... | collective-permute-start | bytes 2064392 | tf_op jit(solution)/shard_map/ppermute | solution.py:16
  158.0 12.6 %collective-permute-start.5 = (f32[96,1792]{1,0:T(8,128)}, f32[96,1792]{1,0:T(8,128)}, u32[]{:S(2)}, u32[]{:S(2)}) collective-permute-start(f32[96,1792]{1,0:T(8,128)} %get-tuple-element.28), channel_id=1, source_target_pairs={{1,0},{2,1},{3,2},{4,3},{5,4},{6,5},{7,6},{8,7},{9,8},{10,9},{11,1... | collective-permute-start | bytes 2064392 | tf_op jit(solution)/shard_map/ppermute | solution.py:19
  168.1 6.0 %copy-start.9 = (bf16[128,896]{1,0:T(8,128)(2,1)S(1)}, bf16[128,896]{1,0:T(8,128)(2,1)}, u32[]{:S(2)}) copy-start(bf16[128,896]{1,0:T(8,128)(2,1)} %copy.30) | copy-start | bytes 688132
  174.1 6.7 %copy-start.5 = (bf16[1,128,1792]{2,1,0:T(8,128)(2,1)S(1)}, bf16[1,128,1792]{2,1,0:T(8,128)(2,1)}, u32[]{:S(2)}) copy-start(bf16[1,128,1792]{2,1,0:T(8,128)(2,1)} %param.19) | copy-start | bytes 1376260
  183.8 9.4 %copy-start.3 = (bf16[320,8,112]{2,1,0:T(8,128)(2,1)S(1)}, bf16[320,8,112]{2,1,0:T(8,128)(2,1)}, u32[]{:S(2)}) copy-start(bf16[320,8,112]{2,1,0:T(8,128)(2,1)} %copy-done.2) | copy-start | bytes 1720324
  183.8 9.4 %copy-start.8 = (bf16[128,896]{0,1:T(8,128)(2,1)S(1)}, bf16[128,896]{0,1:T(8,128)(2,1)}, u32[]{:S(2)}) copy-start(bf16[128,896]{0,1:T(8,128)(2,1)} %copy.22) | copy-start | bytes 688132
  183.8 32.5 %all-to-all-start.1 = ((bf16[32,6,1792]{2,1,0:T(8,128)(2,1)}), bf16[32,6,1792]{2,1,0:T(8,128)(2,1)S(1)}, u32[]{:S(2)}, u32[]{:S(2)}) async-start(bf16[32,6,1792]{2,1,0:T(8,128)(2,1)} %reshape.264), calls=%async_computation.1 | async-start | bytes 1835008 | tf_op jit(solution)/shard_map/all_to_all | solution.py:140
Sparse Core Ops, SparseCore 0:
  10.1 71.1 all-gather.2
  83.4 42.5 all-gather.4
where the time goes:
time: 228 us; the launch traced here: 227 us
  waiting for transfers between devices  105 us (46%)
  starting transfers between devices  36.5 us (16%)
  matrix products  34.7 us (15%)
  local copies, waits for them, and re-layouts  23 us (10%)
  between operations  14.4 us (6%)
  other arithmetic  14.2 us (6%)
    all_gather x1, waiting for transfers between devices, local(): lax.all_gather(out_weight, 'tensor', axis=0, tiled=True)  34 us
    all_gather x1, waiting for transfers between devices, local(): lax.all_gather(qkv_weight, 'tensor', axis=0, tiled=True)  32.5 us
    all_to_all x1, waiting for transfers between devices, local(): lax.all_to_all(back_slots, 'dp', split_axis=0, concat_axis=0, tiled=True)  17.8 us
    all_to_all x1, waiting for transfers between devices, local(): lax.all_to_all(outgoing, 'dp', split_axis=0, concat_axis=0, tiled=True)  13.2 us
    all_to_all x1, starting transfers between devices, local(): lax.all_to_all(outgoing, 'dp', split_axis=0, concat_axis=0, tiled=True)  10.6 us
    ppermute x3, starting transfers between devices, extended(): lax.ppermute(lax.slice_in_dim(block, block.shape[dim] - width, None, axis...  10.1 us
    all_to_all x1, starting transfers between devices, local(): lax.all_to_all(back_slots, 'dp', split_axis=0, concat_axis=0, tiled=True)  9.4 us
    dot_general x1, matrix products, local(): lax.dot_general(grad_proj, full_qkv, (((1,), (1,)), ((), ())), preferred_...  6.63 us
  transfers between devices with their start and end apart: 10, of which 6 were waited for; matrix products, arithmetic and copies ran while one was open for 14% of the time, Pallas kernels for 0%

commit v1 on v0

--- a/solution.py
+++ b/solution.py
@@ -78,7 +78,10 @@
     pick_rows = take_rows[0]
     packed = jnp.take(incoming, pick_rows, axis=0)
     full_qkv, full_out = (
-        lax.all_gather(qkv_weight, "tensor", axis=0, tiled=True),
+        jnp.concatenate(
+            lax.all_to_all(jnp.stack([qkv_weight] * lax.axis_size("tensor")), "tensor", 0, 0),
+            axis=0,
+        ),
         lax.all_gather(out_weight, "tensor", axis=0, tiled=True),
     )
     values, unit_rows, inv_dev, normed = normalize(packed, norm_gain)

time: 228 us -> 403 us (1.77)
  waiting for transfers between devices: 105 us -> 239 us
  blocking collectives: 0 us -> 33.9 us
  local copies, waits for them, and re-layouts: 23 us -> 29.7 us
    ppermute x3, waiting for transfers between devices: 5.77 us -> 221 us  [extended(): lax.ppermute(lax.slice_in_dim(block, 0, width, axis=dim), axis, backward)]
    all_gather x1, waiting for transfers between devices: 34 us -> 0.02 us  [local(): lax.all_gather(out_weight, 'tensor', axis=0, tiled=True)]
    all_to_all x0 -> x1, blocking collectives: none -> 33.9 us  [local(): lax.all_to_all(outgoing, 'dp', split_axis=0, concat_axis=0, tiled=True)]
    all_gather x1 -> x0, waiting for transfers between devices: 32.5 us -> none  [local(): lax.all_gather(qkv_weight, 'tensor', axis=0, tiled=True)]
    all_to_all x1, waiting for transfers between devices: 13.2 us -> 0.01 us  [local(): lax.all_to_all(jnp.stack([qkv_weight] * lax.axis_size('tensor')), 'tensor...]
    another operation x0 -> x1, local copies, waits for them, and re-layouts: none -> 4.35 us  [local(): jnp.stack([qkv_weight] * lax.axis_size('tensor'))]
    all_to_all x1, starting transfers between devices: 9.4 us -> 5.31 us  [local(): lax.all_to_all(back_slots, 'dp', split_axis=0, concat_axis=0, tiled=True)]
  transfers between devices with their start and end apart: 10 -> 9, of which waited for: 6 -> 3; matrix products, arithmetic and copies ran while one was open for 14% -> 7% of each run, Pallas kernels for 0% -> 0%
where the time goes in v1:
time: 403 us; the launch traced here: 401 us
  waiting for transfers between devices  239 us (59%)
  starting transfers between devices  36.5 us (9%)
  matrix products  34.4 us (9%)
  blocking collectives  33.9 us (8%)
  local copies, waits for them, and re-layouts  29.7 us (7%)
  between operations  14.5 us (4%)
  other arithmetic  13.2 us (3%)
    ppermute x3, waiting for transfers between devices, extended(): lax.ppermute(lax.slice_in_dim(block, 0, width, axis=dim), axis, backward)  221 us
    all_to_all x1, blocking collectives, local(): lax.all_to_all(outgoing, 'dp', split_axis=0, concat_axis=0, tiled=True)  33.9 us
    all_to_all x1, waiting for transfers between devices, local(): lax.all_to_all(back_slots, 'dp', split_axis=0, concat_axis=0, tiled=True)  17.2 us
    all_to_all x1, starting transfers between devices, local(): lax.all_to_all(jnp.stack([qkv_weight] * lax.axis_size('tensor')), 'tensor...  13.6 us
    ppermute x3, starting transfers between devices, extended(): lax.ppermute(lax.slice_in_dim(block, block.shape[dim] - width, None, axis...  11.7 us
  transfers between devices with their start and end apart: 9, of which 3 were waited for; matrix products, arithmetic and copies ran while one was open for 7% of the time, Pallas kernels for 0%

profile of v1, /device:TPU:1, one launch (start us, length us, event | category | flops | bytes accessed | tf_op | source)
XLA Modules:
  0.0 400.8 jit_solution(2146544869960887471)
XLA Ops:
  10.5 33.9 %all_to_all.15 = bf16[32,6,1792]{2,1,0:T(8,128)(2,1)S(1)} all-to-all(bf16[32,6,1792]{2,1,0:T(8,128)(2,1)S(1)} %broadcast_select_fusion), channel_id=1, replica_groups=mesh['dp'=32,'tensor'=16] {'dp'}, dimensions={0} | all-to-all | bytes 1376256 | tf_op jit(solution)/shard_map/all_to_all | solution.py:75
  44.4 4.3 %stack.2 = bf16[16,112,2688]{2,1,0:T(8,128)(2,1)} broadcast(bf16[112,2688]{1,0:T(8,128)(2,1)S(1)} %copy-done.7), dimensions={1,2} | broadcast | bytes 10235904 | tf_op jit(solution)/shard_map/stack | solution.py:82
  48.7 13.6 %all-to-all-start.1 = ((bf16[16,112,2688]{2,1,0:T(8,128)(2,1)}), bf16[16,112,2688]{2,1,0:T(8,128)(2,1)}, u32[]{:S(2)}, u32[]{:S(2)}) async-start(bf16[16,112,2688]{2,1,0:T(8,128)(2,1)} %stack.2), calls=%async_computation.1 | async-start | bytes 19267584 | tf_op jit(solution)/shard_map/all_to_all | solution.py:82
  63.1 2.0 collective-permute-start.3
  65.2 3.5 collective-permute-start.2
  68.7 218.1 %collective-permute-done.3 = s32[96]{0:T(128)S(1)} collective-permute-done((s32[96]{0:T(128)S(1)}, s32[96]{0:T(128)S(1)}, u32[]{:S(2)}, u32[]{:S(2)}) %collective-permute-start.3) | collective-permute-done | bytes 416 | tf_op jit(solution)/shard_map/ppermute | solution.py:19
  288.7 5.4 %convolution_convert_fusion = bf16[128,2688]{1,0:T(8,128)(2,1)S(1)} fusion(bf16[1792,2688]{1,0:T(8,128)(2,1)} %bitcast.5, f32[1792]{0:T(1024)S(1)} %copy-done.11, f32[128]{0:T(128)S(1)} %add_rsqrt_fusion, f32[128]{0:T(128)S(1)} %broadcast_multiply_fusion.2, bf16[128,1792]{1,0:T(8,128)(2,1)S(1)} %gather_fusion.1, pred[128]{0:T(512)(128)(4,1)S(1)} %compare_and_fusion.1), kind=kOutput, calls=%fused_computation.6 | convolution fusion | flops 1234845696 | bytes 10788992 | tf_op jit(solution)/shard_map/dot_general | solution.py:88
  295.0 1.9 collective-permute-start.1
  296.9 3.8 collective-permute-start
  300.9 3.0 convolution_convert_fusion.1
  306.9 1.6 reshape.264
  308.9 3.2 fusion.98
  312.1 3.0 convolution_bitcast_fusion
  315.1 3.4 convolution_bitcast_fusion.1
  318.5 2.1 copy.28
  322.0 1.4 constant_dynamic-update-slice_fusion.1
  323.6 1.9 copy.29
  325.5 2.6 reshape.269
  330.7 4.4 %collective-permute-start.4 = (f32[96,1792]{1,0:T(8,128)}, f32[96,1792]{1,0:T(8,128)}, u32[]{:S(2)}, u32[]{:S(2)}) collective-permute-start(f32[96,1792]{1,0:T(8,128)} %get-tuple-element.29), channel_id=1, source_target_pairs={{0,1},{1,2},{2,3},{3,4},{4,5},{5,6},{6,7},{7,8},{8,9},{9,10},{10,1... | collective-permute-start | bytes 2064392 | tf_op jit(solution)/shard_map/ppermute | solution.py:16
  336.1 1.9 collective-permute-start.5
  338.0 4.2 %fusion.17 = bf16[8,112,128]{2,1,0:T(8,128)(2,1)} fusion(f32[8,128,320]{1,2,0:T(8,128)} %copy-done.6, bf16[320,8,112]{2,1,0:T(8,128)(2,1)} %reshape.264, f32[8,128,320]{1,2,0:T(8,128)} %get-tuple-element.41, f32[8,128]{1,0:T(8,128)S(1)} %get-tuple-element.40), kind=kOutput, calls=%fused_computation.27 | convolution fusion | flops 75810112 | bytes 3428352 | tf_op jit(solution)/shard_map/hqk,khd->qhd/dot_general | solution.py:111
  342.2 1.8 copy.30
  344.0 2.0 fusion.33
  346.0 2.7 collective-permute-done.5
  348.7 2.3 fusion.32
  352.2 6.6 %fusion.94 = (f32[128]{0:T(128)S(1)}, f32[128]{0:T(128)S(1)}, f32[128,1792]{1,0:T(8,128)S(1)}) fusion(f32[128]{0:T(128)S(1)} %add_rsqrt_fusion, f32[128]{0:T(128)S(1)} %broadcast_multiply_fusion.2, bf16[128,1792]{1,0:T(8,128)(2,1)S(1)} %gather_fusion.1, pred[128]{0:T(512)(128)(4,1)S(1)} %compare_and_fusion.1, f32[1792]{0:T(1024)S(1)} %copy-done.11, ...), kind=kOutput, calls=%fused_computation.107 | convolution fusion | flops 1236336384 | bytes 11707520 | tf_op jit(solution)/shard_map/dot_general | solution.py:129
  358.8 1.9 scatter_custom_fusion
  361.9 5.3 %all-to-all-start.2 = ((bf16[32,6,1792]{2,1,0:T(8,128)(2,1)}), bf16[32,6,1792]{2,1,0:T(8,128)(2,1)S(1)}, u32[]{:S(2)}, u32[]{:S(2)}) async-start(bf16[32,6,1792]{2,1,0:T(8,128)(2,1)} %reshape.270), calls=%async_computation.2 | async-start | bytes 1835008 | tf_op jit(solution)/shard_map/all_to_all | solution.py:143
  367.2 2.0 convolution_convert_fusion.2
  369.2 3.4 fusion.3
  372.5 17.2 %all-to-all-done.2 = bf16[32,6,1792]{2,1,0:T(8,128)(2,1)S(1)} async-done(((bf16[32,6,1792]{2,1,0:T(8,128)(2,1)}), bf16[32,6,1792]{2,1,0:T(8,128)(2,1)S(1)}, u32[]{:S(2)}, u32[]{:S(2)}) %all-to-all-start.2) | async-done | bytes 688160 | tf_op jit(solution)/shard_map/all_to_all | solution.py:143
  389.9 3.1 scatter_custom_fusion.1
  (76 shorter events, 19.0 us)
Async XLA Ops:
  7.2 1.7 copy-start
  10.5 33.9 %copy-start.7 = (bf16[112,2688]{1,0:T(8,128)(2,1)S(1)}, bf16[112,2688]{1,0:T(8,128)(2,1)}, u32[]{:S(2)}) copy-start(bf16[112,2688]{1,0:T(8,128)(2,1)} %param.17) | copy-start | bytes 1806340
  48.7 14.3 %copy-start.12 = (s32[1,128]{1,0:T(1,128)S(1)}, s32[1,128]{1,0:T(1,128)}, u32[]{:S(2)}) copy-start(s32[1,128]{1,0:T(1,128)} %param.15) | copy-start | bytes 1540
  48.7 20.0 %copy-start.13 = (s32[1,128]{1,0:T(1,128)S(1)}, s32[1,128]{1,0:T(1,128)}, u32[]{:S(2)}) copy-start(s32[1,128]{1,0:T(1,128)} %param.14) | copy-start | bytes 1540
  48.7 239.9 %all-to-all-start.1 = ((bf16[16,112,2688]{2,1,0:T(8,128)(2,1)}), bf16[16,112,2688]{2,1,0:T(8,128)(2,1)}, u32[]{:S(2)}, u32[]{:S(2)}) async-start(bf16[16,112,2688]{2,1,0:T(8,128)(2,1)} %stack.2), calls=%async_computation.1 | async-start | bytes 19267584 | tf_op jit(solution)/shard_map/all_to_all | solution.py:82
  62.3 238.6 %all-gather.2.cloned.1.call-start = ((), (), s32[]{:S(2)}) async-start(), calls=%async_computation.3 | async-start | bytes 3411968 | tf_op jit(solution)/shard_map/all_gather | solution.py:85
  63.1 223.7 %collective-permute-start.3 = (s32[96]{0:T(128)S(1)}, s32[96]{0:T(128)S(1)}, u32[]{:S(2)}, u32[]{:S(2)}) collective-permute-start(s32[96]{0:T(128)S(1)} %get-tuple-element.37), channel_id=1, source_target_pairs={{1,0},{2,1},{3,2},{4,3},{5,4},{6,5},{7,6},{8,7},{9,8},{10,9},{11,1... | collective-permute-start | bytes 1160 | tf_op jit(solution)/shard_map/ppermute | solution.py:19
  65.2 221.7 %collective-permute-start.2 = (s32[96]{0:T(128)S(1)}, s32[96]{0:T(128)S(1)}, u32[]{:S(2)}, u32[]{:S(2)}) collective-permute-start(s32[96]{0:T(128)S(1)} %get-tuple-element.36), channel_id=1, source_target_pairs={{0,1},{1,2},{2,3},{3,4},{4,5},{5,6},{6,7},{7,8},{8,9},{9,10},{10,1... | collective-permute-start | bytes 1160 | tf_op jit(solution)/shard_map/ppermute | solution.py:16
  287.1 1.5 copy-start.11
  294.1 6.8 %copy-start.3 = (bf16[1,128,1792]{2,1,0:T(8,128)(2,1)S(1)}, bf16[1,128,1792]{2,1,0:T(8,128)(2,1)}, u32[]{:S(2)}) copy-start(bf16[1,128,1792]{2,1,0:T(8,128)(2,1)} %param.19) | copy-start | bytes 1376260
  295.0 10.0 %collective-permute-start.1 = (bf16[96,1792]{1,0:T(8,128)(2,1)}, bf16[96,1792]{1,0:T(8,128)(2,1)S(1)}, u32[]{:S(2)}, u32[]{:S(2)}) collective-permute-start(bf16[96,1792]{1,0:T(8,128)(2,1)} %get-tuple-element.33), channel_id=1, source_target_pairs={{1,0},{2,1},{3,2},{4,3},{5,4},{6,5},{7,6},{8,7},{9,8},{10,9},{11,1... | collective-permute-start | bytes 1032200 | tf_op jit(solution)/shard_map/ppermute | solution.py:19
  296.9 8.1 %collective-permute-start = (bf16[96,1792]{1,0:T(8,128)(2,1)}, bf16[96,1792]{1,0:T(8,128)(2,1)}, u32[]{:S(2)}, u32[]{:S(2)}) collective-permute-start(bf16[96,1792]{1,0:T(8,128)(2,1)} %get-tuple-element.32), channel_id=1, source_target_pairs={{0,1},{1,2},{2,3},{3,4},{4,5},{5,6},{6,7},{7,8},{8,9},{9,10},{10,1... | collective-permute-start | bytes 1032200 | tf_op jit(solution)/shard_map/ppermute | solution.py:16
  306.9 1.9 copy-start.1
  308.9 6.2 %copy-start.6 = (f32[8,128,320]{1,2,0:T(8,128)}, f32[8,128,320]{1,2,0:T(8,128)S(1)}, u32[]{:S(2)}) copy-start(f32[8,128,320]{1,2,0:T(8,128)S(1)} %fusion.41) | copy-start | bytes 3932164
  308.9 3.2 copy-start.8
  322.0 1.7 copy-start.5
  330.7 13.3 %collective-permute-start.4 = (f32[96,1792]{1,0:T(8,128)}, f32[96,1792]{1,0:T(8,128)}, u32[]{:S(2)}, u32[]{:S(2)}) collective-permute-start(f32[96,1792]{1,0:T(8,128)} %get-tuple-element.29), channel_id=1, source_target_pairs={{0,1},{1,2},{2,3},{3,4},{4,5},{5,6},{6,7},{7,8},{8,9},{9,10},{10,1... | collective-permute-start | bytes 2064392 | tf_op jit(solution)/shard_map/ppermute | solution.py:16
  336.1 12.6 %collective-permute-start.5 = (f32[96,1792]{1,0:T(8,128)}, f32[96,1792]{1,0:T(8,128)}, u32[]{:S(2)}, u32[]{:S(2)}) collective-permute-start(f32[96,1792]{1,0:T(8,128)} %get-tuple-element.28), channel_id=1, source_target_pairs={{1,0},{2,1},{3,2},{4,3},{5,4},{6,5},{7,6},{8,7},{9,8},{10,9},{11,1... | collective-permute-start | bytes 2064392 | tf_op jit(solution)/shard_map/ppermute | solution.py:19
  346.0 6.2 %copy-start.10 = (bf16[128,896]{1,0:T(8,128)(2,1)S(1)}, bf16[128,896]{1,0:T(8,128)(2,1)}, u32[]{:S(2)}) copy-start(bf16[128,896]{1,0:T(8,128)(2,1)} %copy.30) | copy-start | bytes 688132
  352.2 6.7 %copy-start.4 = (bf16[1,128,1792]{2,1,0:T(8,128)(2,1)S(1)}, bf16[1,128,1792]{2,1,0:T(8,128)(2,1)}, u32[]{:S(2)}) copy-start(bf16[1,128,1792]{2,1,0:T(8,128)(2,1)} %param.19) | copy-start | bytes 1376260
  361.9 5.3 %copy-start.2 = (bf16[320,8,112]{2,1,0:T(8,128)(2,1)S(1)}, bf16[320,8,112]{2,1,0:T(8,128)(2,1)}, u32[]{:S(2)}) copy-start(bf16[320,8,112]{2,1,0:T(8,128)(2,1)} %copy-done.1) | copy-start | bytes 1720324
  361.9 5.3 %copy-start.9 = (bf16[128,896]{0,1:T(8,128)(2,1)S(1)}, bf16[128,896]{0,1:T(8,128)(2,1)}, u32[]{:S(2)}) copy-start(bf16[128,896]{0,1:T(8,128)(2,1)} %copy.22) | copy-start | bytes 688132
  361.9 27.8 %all-to-all-start.2 = ((bf16[32,6,1792]{2,1,0:T(8,128)(2,1)}), bf16[32,6,1792]{2,1,0:T(8,128)(2,1)S(1)}, u32[]{:S(2)}, u32[]{:S(2)}) async-start(bf16[32,6,1792]{2,1,0:T(8,128)(2,1)} %reshape.270), calls=%async_computation.2 | async-start | bytes 1835008 | tf_op jit(solution)/shard_map/all_to_all | solution.py:143
Sparse Core Ops, SparseCore 0:
  65.2 85.6 all-gather.1
